TPU v7x, 512 devices: a whole 4x8x8 slice. The times are simulated.
512 devices in a mesh: seq: 64 (over z_hi, y, core), ch: 8 (over x, z_lo).
Axes of the slice: x: 4, y: 8, z: 8 (z_hi: 4, z_lo: 2; z = z_hi * 2 + z_lo), core: 2. Of those that a mesh axis runs over, the one named last changes fastest.
Arguments:
- inputs: bfloat16 [262144, 2048], P('seq', 'ch'), may hold values from -6 to 6
- first_factor: bfloat16 [512, 512], P('ch'), may hold values from -0.25 to 0.25
- twiddle: float32 [512, 512], P('seq'), may hold values from -4 to 4
- second_factor: bfloat16 [512, 512], P('ch'), may hold values from -0.25 to 0.25
- block_first: bfloat16 [64, 32, 32], P('ch'), may hold values from -1 to 1
- block_second: bfloat16 [32, 64, 64], P('ch'), may hold values from -0.75 to 0.75
Outputs:
- mixed_out: bfloat16 [262144, 2048], P('seq', 'ch')
All inputs are finite; a program needn't handle non-finite values.
Results may differ from a plain program's by a relative error of at most 0.007.
Values may be sent and summed in bfloat16 or wider, within the bound.
No kernel may reach another device: no remote copies, remote signals or barrier semaphores. Data moves between devices by JAX's collectives and lax.ppermute only.
A program may use at most 128 MiB of HBM per device.

v0:
```python
import jax
import jax.numpy as jnp
from jax import lax
from jax.sharding import PartitionSpec as P

BLOCK = 512
CHUNKS = 2


def channel_weights(block_first, block_second, n_ch):
    n_a, n_m, n_b = block_first.shape
    m_l = n_m // n_ch
    bf = jnp.transpose(block_first, (1, 0, 2))
    bf = bf.reshape(n_ch, m_l, n_a, 1, n_b)
    eye_a = jnp.eye(n_a, dtype=jnp.bool_).reshape(1, 1, n_a, n_a, 1)
    w1t = jnp.where(eye_a, bf, jnp.zeros((), bf.dtype))
    w1t = w1t.reshape(n_ch * m_l * n_a, n_a * n_b)
    n_m2, n_p, n_a2 = block_second.shape
    a_l = n_a2 // n_ch
    bs = block_second.reshape(n_m2, n_p, n_ch, a_l)
    bs = jnp.transpose(bs, (2, 0, 3, 1))
    bs = bs.reshape(n_ch, n_m2, a_l, 1, n_p)
    eye_m = jnp.eye(n_m2, dtype=jnp.bool_).reshape(1, n_m2, 1, n_m2, 1)
    w2 = jnp.where(eye_m, bs, jnp.zeros((), bs.dtype))
    w2 = w2.reshape(n_ch * n_m2 * a_l, n_m2 * n_p)
    return (w1t, w2)


def make_local(n_seq, n_ch):

    def local(inputs, first_factor, twiddle, second_factor, block_first, block_second):
        tok_rows, channels = inputs.shape
        outer_rows = tok_rows // BLOCK
        token_grid = inputs.reshape(outer_rows, BLOCK, channels)
        rows = first_factor.shape[0]
        both = lax.all_gather(
            jnp.concatenate([first_factor, second_factor], axis=0), "ch", axis=0, tiled=True
        ).reshape(n_ch, 2, rows, BLOCK)
        full_first = both[:, 0].reshape(BLOCK, BLOCK)
        full_second = both[:, 1].reshape(BLOCK, BLOCK)
        twiddle_t = jnp.transpose(twiddle)
        w1t, w2 = channel_weights(block_first, block_second, n_ch)
        contract = (((1,), (1,)), ((), ()))
        width = BLOCK // CHUNKS
        outs = []
        for q in range(CHUNKS):
            lo = q * width
            first = lax.dot_general(
                full_first[lo : lo + width],
                token_grid,
                contract,
                preferred_element_type=jnp.float32,
            )
            twisted = (first * twiddle_t[lo : lo + width, :, None]).astype(jnp.bfloat16)
            gathered = lax.all_to_all(twisted, "seq", split_axis=0, concat_axis=1, tiled=True)
            mixed = lax.dot_general(
                full_second, gathered, contract, preferred_element_type=jnp.float32
            ).astype(jnp.bfloat16)
            returned = lax.all_to_all(mixed, "seq", split_axis=0, concat_axis=1, tiled=True)
            gated = (
                token_grid[:, lo : lo + width].astype(jnp.float32) * returned.astype(jnp.float32)
            ).astype(jnp.bfloat16)
            gated = gated.reshape(outer_rows * width, channels)
            middle_t = lax.dot_general(
                w1t, gated, contract, preferred_element_type=jnp.float32
            ).astype(jnp.bfloat16)
            middle_t = middle_t.reshape(n_ch, channels // n_ch, outer_rows * width)
            recv = lax.all_to_all(middle_t, "ch", split_axis=0, concat_axis=0, tiled=True)
            recv = recv.reshape(channels, outer_rows * width)
            result = lax.dot_general(
                recv, w2, (((0,), (0,)), ((), ())), preferred_element_type=jnp.float32
            ).astype(jnp.bfloat16)
            outs.append(result.reshape(outer_rows, width, channels))
        out = jnp.concatenate(outs, axis=1)
        return out.reshape(tok_rows, channels)

    return local


def solution(mesh):
    placed = (
        P("seq", "ch"),
        P("ch", None),
        P("seq", None),
        P("ch", None),
        P("ch", None, None),
        P("ch", None, None),
    )
    return jax.shard_map(
        make_local(mesh.shape["seq"], mesh.shape["ch"]),
        mesh=mesh,
        in_specs=placed,
        out_specs=P("seq", "ch"),
        check_vma=False,
    )
```

profile of v0, /device:TPU:24, one launch (start us, length us, event | category | flops | bytes accessed | tf_op | source)
XLA Modules:
  0.0 274.9 jit_solution(7449750613190882592)
XLA Ops:
  6.5 1.5 pad_maximum_fusion.1
  8.8 51.1 %all-gather.2.cloned.1.call-done = bf16[1024,512]{1,0:T(8,128)(2,1)} async-done(((bf16[128,512]{1,0:T(8,128)(2,1)}), bf16[1024,512]{1,0:T(8,128)(2,1)}) %all-gather.2.cloned.1.call-update) | async-done | bytes 1048592 | tf_op jit(solution)/shard_map/all_gather | solution.py:36
  61.0 2.3 multiply_convert_fusion.3
  63.3 1.6 copy.29
  64.9 12.4 %all-to-all-start = ((bf16[256,8,256]{2,1,0:T(8,128)(2,1)}), bf16[256,8,256]{2,1,0:T(8,128)(2,1)S(1)}, u32[]{:S(2)}, u32[]{:S(2)}) async-start(bf16[256,8,256]{2,1,0:T(8,128)(2,1)} %copy.29), calls=%async_computation | async-start | bytes 2097152 | tf_op jit(solution)/shard_map/all_to_all | solution.py:55
  78.0 1.6 copy.36
  79.6 25.8 %all-to-all-done = bf16[256,8,256]{2,1,0:T(8,128)(2,1)S(1)} async-done(((bf16[256,8,256]{2,1,0:T(8,128)(2,1)}), bf16[256,8,256]{2,1,0:T(8,128)(2,1)S(1)}, u32[]{:S(2)}, u32[]{:S(2)}) %all-to-all-start) | async-done | bytes 1048608 | tf_op jit(solution)/shard_map/all_to_all | solution.py:55
  105.4 8.5 %all-to-all-start.3 = ((bf16[256,8,256]{2,1,0:T(8,128)(2,1)}), bf16[256,8,256]{2,1,0:T(8,128)(2,1)S(1)}, u32[]{:S(2)}, u32[]{:S(2)}) async-start(bf16[256,8,256]{2,1,0:T(8,128)(2,1)} %copy.36), calls=%async_computation.3 | async-start | bytes 2097152 | tf_op jit(solution)/shard_map/all_to_all | solution.py:55
  115.5 1.8 copy.31
  117.2 25.0 %all-to-all-done.3 = bf16[256,8,256]{2,1,0:T(8,128)(2,1)S(1)} async-done(((bf16[256,8,256]{2,1,0:T(8,128)(2,1)}), bf16[256,8,256]{2,1,0:T(8,128)(2,1)S(1)}, u32[]{:S(2)}, u32[]{:S(2)}) %all-to-all-start.3) | async-done | bytes 1048608 | tf_op jit(solution)/shard_map/all_to_all | solution.py:55
  142.2 9.0 %all-to-all-start.1 = ((bf16[512,4,256]{2,1,0:T(4,128)(2,1)}), bf16[512,4,256]{2,1,0:T(4,128)(2,1)S(1)}, u32[]{:S(2)}, u32[]{:S(2)}) async-start(bf16[512,4,256]{2,1,0:T(4,128)(2,1)} %copy.31), calls=%async_computation.1 | async-start | bytes 2097152 | tf_op jit(solution)/shard_map/all_to_all | solution.py:59
  151.9 1.8 copy.38
  153.8 25.7 %all-to-all-done.1 = bf16[512,4,256]{2,1,0:T(4,128)(2,1)S(1)} async-done(((bf16[512,4,256]{2,1,0:T(4,128)(2,1)}), bf16[512,4,256]{2,1,0:T(4,128)(2,1)S(1)}, u32[]{:S(2)}, u32[]{:S(2)}) %all-to-all-start.1) | async-done | bytes 1048608 | tf_op jit(solution)/shard_map/all_to_all | solution.py:59
  179.5 9.3 %all-to-all-start.4 = ((bf16[512,4,256]{2,1,0:T(4,128)(2,1)}), bf16[512,4,256]{2,1,0:T(4,128)(2,1)S(1)}, u32[]{:S(2)}, u32[]{:S(2)}) async-start(bf16[512,4,256]{2,1,0:T(4,128)(2,1)} %copy.38), calls=%async_computation.4 | async-start | bytes 2097152 | tf_op jit(solution)/shard_map/all_to_all | solution.py:59
  190.0 1.7 reshape.114
  191.7 25.3 %all-to-all-done.4 = bf16[512,4,256]{2,1,0:T(4,128)(2,1)S(1)} async-done(((bf16[512,4,256]{2,1,0:T(4,128)(2,1)}), bf16[512,4,256]{2,1,0:T(4,128)(2,1)S(1)}, u32[]{:S(2)}, u32[]{:S(2)}) %all-to-all-start.4) | async-done | bytes 1048608 | tf_op jit(solution)/shard_map/all_to_all | solution.py:59
  217.7 1.7 reshape.115
  219.4 3.4 %multiply_convert_fusion.2 = (bf16[8,256,256]{2,1,0:T(8,128)(2,1)S(1)}, bf16[8,256,256]{2,1,0:T(8,128)(2,1)S(1)}) fusion(f32[8,256,256]{2,1,0:T(8,128)} %reshape.114, bf16[8,512,256]{2,1,0:T(8,128)(2,1)} %bitcast.81, f32[8,256,256]{2,1,0:T(8,128)} %reshape.115), kind=kLoop, calls=%fused_computation.9 | loop fusion | flops 3145728 | bytes 8388608 | tf_op jit(solution)/shard_map/convert_element_type | solution.py:62
  222.8 1.5 convolution_convert_fusion.3
  224.3 5.2 %all-to-all-start.2 = ((bf16[8,32,2048]{2,1,0:T(8,128)(2,1)}), bf16[8,32,2048]{2,1,0:T(8,128)(2,1)S(1)}, u32[]{:S(2)}, u32[]{:S(2)}) async-start(bf16[8,32,2048]{2,1,0:T(8,128)(2,1)} %bitcast.15), calls=%async_computation.2 | async-start | bytes 2097152 | tf_op jit(solution)/shard_map/all_to_all | solution.py:68
  230.9 15.0 %all-to-all-done.2 = bf16[8,32,2048]{2,1,0:T(8,128)(2,1)S(1)} async-done(((bf16[8,32,2048]{2,1,0:T(8,128)(2,1)}), bf16[8,32,2048]{2,1,0:T(8,128)(2,1)S(1)}, u32[]{:S(2)}, u32[]{:S(2)}) %all-to-all-start.2) | async-done | bytes 1048608 | tf_op jit(solution)/shard_map/all_to_all | solution.py:68
  245.9 3.6 %all-to-all-start.5 = ((bf16[8,32,2048]{2,1,0:T(8,128)(2,1)}), bf16[8,32,2048]{2,1,0:T(8,128)(2,1)S(1)}, u32[]{:S(2)}, u32[]{:S(2)}) async-start(bf16[8,32,2048]{2,1,0:T(8,128)(2,1)} %bitcast.29), calls=%async_computation.5 | async-start | bytes 2097152 | tf_op jit(solution)/shard_map/all_to_all | solution.py:68
  250.5 15.6 %all-to-all-done.5 = bf16[8,32,2048]{2,1,0:T(8,128)(2,1)S(1)} async-done(((bf16[8,32,2048]{2,1,0:T(8,128)(2,1)}), bf16[8,32,2048]{2,1,0:T(8,128)(2,1)S(1)}, u32[]{:S(2)}, u32[]{:S(2)}) %all-to-all-start.5) | async-done | bytes 1048608 | tf_op jit(solution)/shard_map/all_to_all | solution.py:68
  266.6 1.5 pad_maximum_fusion
  (35 shorter events, 9.6 us)
Async XLA Ops:
  6.5 53.4 %all-gather.2.cloned.1.call-start = ((), (), s32[]{:S(2)}) async-start(), calls=%async_computation.6 | async-start | bytes 1179648 | tf_op jit(solution)/shard_map/all_gather | solution.py:36
  63.3 14.0 %copy-start = (bf16[4096,256]{1,0:T(8,128)(2,1)S(1)}, bf16[4096,256]{1,0:T(8,128)(2,1)}, u32[]{:S(2)}) copy-start(bf16[4096,256]{1,0:T(8,128)(2,1)} %param.6) | copy-start | bytes 6291460
  64.9 40.5 %all-to-all-start = ((bf16[256,8,256]{2,1,0:T(8,128)(2,1)}), bf16[256,8,256]{2,1,0:T(8,128)(2,1)S(1)}, u32[]{:S(2)}, u32[]{:S(2)}) async-start(bf16[256,8,256]{2,1,0:T(8,128)(2,1)} %copy.29), calls=%async_computation | async-start | bytes 2097152 | tf_op jit(solution)/shard_map/all_to_all | solution.py:55
  78.0 35.8 %copy-start.1 = (bf16[1024,512]{1,0:T(8,128)(2,1)S(1)}, bf16[1024,512]{1,0:T(8,128)(2,1)}, u32[]{:S(2)}) copy-start(bf16[1024,512]{1,0:T(8,128)(2,1)} %all-gather.2.cloned.1.call-done) | copy-start | bytes 3145732
  105.4 36.8 %all-to-all-start.3 = ((bf16[256,8,256]{2,1,0:T(8,128)(2,1)}), bf16[256,8,256]{2,1,0:T(8,128)(2,1)S(1)}, u32[]{:S(2)}, u32[]{:S(2)}) async-start(bf16[256,8,256]{2,1,0:T(8,128)(2,1)} %copy.36), calls=%async_computation.3 | async-start | bytes 2097152 | tf_op jit(solution)/shard_map/all_to_all | solution.py:55
  113.9 0.8 copy-start.2
  115.4 35.8 %copy-start.3 = (bf16[8,1,64,512]{3,2,1,0:T(8,128)(2,1)S(1)}, bf16[8,1,64,512]{3,2,1,0:T(8,128)(2,1)}, u32[]{:S(2)}) copy-start(bf16[8,1,64,512]{3,2,1,0:T(8,128)(2,1)} %copy-done.2) | copy-start | bytes 1572868
  142.2 37.2 %all-to-all-start.1 = ((bf16[512,4,256]{2,1,0:T(4,128)(2,1)}), bf16[512,4,256]{2,1,0:T(4,128)(2,1)S(1)}, u32[]{:S(2)}, u32[]{:S(2)}) async-start(bf16[512,4,256]{2,1,0:T(4,128)(2,1)} %copy.31), calls=%async_computation.1 | async-start | bytes 2097152 | tf_op jit(solution)/shard_map/all_to_all | solution.py:59
  151.9 36.8 %copy-start.4 = (bf16[8,32,32]{2,1,0:T(8,128)(2,1)S(1)}, bf16[8,32,32]{2,1,0:T(8,128)(2,1)}, u32[]{:S(2)}) copy-start(bf16[8,32,32]{2,1,0:T(8,128)(2,1)} %param.10) | copy-start | bytes 49156
  179.5 37.5 %all-to-all-start.4 = ((bf16[512,4,256]{2,1,0:T(4,128)(2,1)}), bf16[512,4,256]{2,1,0:T(4,128)(2,1)S(1)}, u32[]{:S(2)}, u32[]{:S(2)}) async-start(bf16[512,4,256]{2,1,0:T(4,128)(2,1)} %copy.38), calls=%async_computation.4 | async-start | bytes 2097152 | tf_op jit(solution)/shard_map/all_to_all | solution.py:59
  224.3 21.6 %all-to-all-start.2 = ((bf16[8,32,2048]{2,1,0:T(8,128)(2,1)}), bf16[8,32,2048]{2,1,0:T(8,128)(2,1)S(1)}, u32[]{:S(2)}, u32[]{:S(2)}) async-start(bf16[8,32,2048]{2,1,0:T(8,128)(2,1)} %bitcast.15), calls=%async_computation.2 | async-start | bytes 2097152 | tf_op jit(solution)/shard_map/all_to_all | solution.py:68
  229.5 20.0 %copy-start.5 = (bf16[4,64,64]{2,1,0:T(8,128)(2,1)S(1)}, bf16[4,64,64]{2,1,0:T(8,128)(2,1)}, u32[]{:S(2)}) copy-start(bf16[4,64,64]{2,1,0:T(8,128)(2,1)} %param.11) | copy-start | bytes 98308
  245.9 20.2 %all-to-all-start.5 = ((bf16[8,32,2048]{2,1,0:T(8,128)(2,1)}), bf16[8,32,2048]{2,1,0:T(8,128)(2,1)S(1)}, u32[]{:S(2)}, u32[]{:S(2)}) async-start(bf16[8,32,2048]{2,1,0:T(8,128)(2,1)} %bitcast.29), calls=%async_computation.5 | async-start | bytes 2097152 | tf_op jit(solution)/shard_map/all_to_all | solution.py:68
Sparse Core Ops, SparseCore 0:
  9.4 50.4 all-gather.1
where the time goes:
time: 276 us; the launch traced here: 275 us
  waiting for transfers between devices  183 us (66%)
  starting transfers between devices  47.9 us (17%)
  local copies, waits for them, and re-layouts  14.3 us (5%)
  between operations  13.7 us (5%)
  matrix products  8.32 us (3%)
  other arithmetic  7.35 us (3%)
    all_gather x1, waiting for transfers between devices, local(): lax.all_gather(jnp.concatenate([first_factor, second_factor], axis=0), 'c...  51.1 us
    all_to_all x2, waiting for transfers between devices, local(): lax.all_to_all(mixed, 'seq', split_axis=0, concat_axis=1, tiled=True)  51 us
    all_to_all x2, waiting for transfers between devices, local(): lax.all_to_all(twisted, 'seq', split_axis=0, concat_axis=1, tiled=True)  50.8 us
    all_to_all x2, waiting for transfers between devices, local(): lax.all_to_all(middle_t, 'ch', split_axis=0, concat_axis=0, tiled=True)  30.6 us
    all_to_all x2, starting transfers between devices, local(): lax.all_to_all(twisted, 'seq', split_axis=0, concat_axis=1, tiled=True)  20.9 us
    all_to_all x2, starting transfers between devices, local(): lax.all_to_all(mixed, 'seq', split_axis=0, concat_axis=1, tiled=True)  18.2 us
    all_to_all x2, starting transfers between devices, local(): lax.all_to_all(middle_t, 'ch', split_axis=0, concat_axis=0, tiled=True)  8.74 us
  transfers between devices with their start and end apart: 7, of which 7 were waited for; matrix products, arithmetic and copies ran while one was open for 5% of the time, Pallas kernels for 0%

commit v1 on v0

--- a/solution.py
+++ b/solution.py
@@ -2,9 +2,16 @@
 import jax.numpy as jnp
 from jax import lax
 from jax.sharding import PartitionSpec as P
+from jax.lax import all_to_all, psum
 
 BLOCK = 512
 CHUNKS = 2
+
+
+def create_tails(x_local):
+    return jnp.concatenate(
+        all_to_all(jnp.stack([x_local for _ in range(psum(1, "ch"))]), "ch", 0, 0), 0
+    )
 
 
 def channel_weights(block_first, block_second, n_ch):
@@ -33,9 +40,9 @@
         outer_rows = tok_rows // BLOCK
         token_grid = inputs.reshape(outer_rows, BLOCK, channels)
         rows = first_factor.shape[0]
-        both = lax.all_gather(
-            jnp.concatenate([first_factor, second_factor], axis=0), "ch", axis=0, tiled=True
-        ).reshape(n_ch, 2, rows, BLOCK)
+        both = create_tails(jnp.concatenate([first_factor, second_factor], axis=0)).reshape(
+            n_ch, 2, rows, BLOCK
+        )
         full_first = both[:, 0].reshape(BLOCK, BLOCK)
         full_second = both[:, 1].reshape(BLOCK, BLOCK)
         twiddle_t = jnp.transpose(twiddle)

time: 276 us -> 233 us (0.84)
  waiting for transfers between devices: 183 us -> 148 us
  between operations: 13.7 us -> 0.26 us
  starting transfers between devices: 47.9 us -> 57.3 us
    all_gather x1 -> x0, waiting for transfers between devices: 51.1 us -> none  [local(): lax.all_gather(jnp.concatenate([first_factor, second_factor], axis=0), 'c...]
    all_to_all x0 -> x1, waiting for transfers between devices: none -> 15.7 us  [create_tails(): all_to_all(jnp.stack([x_local for _ in range(psum(1, 'ch'))]), 'ch', 0, 0)]
    all_to_all x0 -> x1, starting transfers between devices: none -> 6.11 us  [create_tails(): all_to_all(jnp.stack([x_local for _ in range(psum(1, 'ch'))]), 'ch', 0, 0)]
    all_to_all x2, starting transfers between devices: 20.9 us -> 25.1 us  [local(): lax.all_to_all(twisted, 'seq', split_axis=0, concat_axis=1, tiled=True)]
  transfers between devices with their start and end apart: 7 -> 7, of which waited for: 7 -> 7; matrix products, arithmetic and copies ran while one was open for 5% -> 6% of each run, Pallas kernels for 0% -> 0%
where the time goes in v1:
time: 233 us
  waiting for transfers between devices  148 us (64%)
  starting transfers between devices  57.3 us (25%)
  local copies, waits for them, and re-layouts  12.8 us (5%)
  matrix products  7.94 us (3%)
  other arithmetic  6.71 us (3%)
    all_to_all x2, waiting for transfers between devices, local(): lax.all_to_all(mixed, 'seq', split_axis=0, concat_axis=1, tiled=True)  51.2 us
    all_to_all x2, waiting for transfers between devices, local(): lax.all_to_all(twisted, 'seq', split_axis=0, concat_axis=1, tiled=True)  50.4 us
    all_to_all x2, waiting for transfers between devices, local(): lax.all_to_all(middle_t, 'ch', split_axis=0, concat_axis=0, tiled=True)  30.5 us
    all_to_all x2, starting transfers between devices, local(): lax.all_to_all(twisted, 'seq', split_axis=0, concat_axis=1, tiled=True)  25.1 us
    all_to_all x2, starting transfers between devices, local(): lax.all_to_all(mixed, 'seq', split_axis=0, concat_axis=1, tiled=True)  19 us
    all_to_all x1, waiting for transfers between devices, create_tails(): all_to_all(jnp.stack([x_local for _ in range(psum(1, 'ch'))]), 'ch', 0, 0)  15.7 us
    all_to_all x2, starting transfers between devices, local(): lax.all_to_all(middle_t, 'ch', split_axis=0, concat_axis=0, tiled=True)  7.12 us
    all_to_all x1, starting transfers between devices, create_tails(): all_to_all(jnp.stack([x_local for _ in range(psum(1, 'ch'))]), 'ch', 0, 0)  6.11 us
  transfers between devices with their start and end apart: 7, of which 7 were waited for; matrix products, arithmetic and copies ran while one was open for 6% of the time, Pallas kernels for 0%

profile of v1, /device:TPU:24, one launch (start us, length us, event | category | flops | bytes accessed | tf_op | source)
XLA Modules:
  0.0 232.8 jit_solution(8422021919565129018)
XLA Ops:
  2.0 6.1 %all-to-all-start = ((bf16[8,128,512]{2,1,0:T(8,128)(2,1)}), bf16[8,128,512]{2,1,0:T(8,128)(2,1)S(1)}, u32[]{:S(2)}, u32[]{:S(2)}) async-start(bf16[8,128,512]{2,1,0:T(8,128)(2,1)} %stack.2), calls=%async_computation | async-start | bytes 2097152 | tf_op jit(solution)/shard_map/all_to_all | solution.py:13
  8.1 15.7 %all-to-all-done = bf16[8,128,512]{2,1,0:T(8,128)(2,1)S(1)} async-done(((bf16[8,128,512]{2,1,0:T(8,128)(2,1)}), bf16[8,128,512]{2,1,0:T(8,128)(2,1)S(1)}, u32[]{:S(2)}, u32[]{:S(2)}) %all-to-all-start) | async-done | bytes 1048608 | tf_op jit(solution)/shard_map/all_to_all | solution.py:13
  24.6 1.6 copy.27
  26.1 15.6 %all-to-all-start.4 = ((bf16[256,8,256]{2,1,0:T(8,128)(2,1)}), bf16[256,8,256]{2,1,0:T(8,128)(2,1)}, u32[]{:S(2)}, u32[]{:S(2)}) async-start(bf16[256,8,256]{2,1,0:T(8,128)(2,1)} %copy.27), calls=%async_computation.4 | async-start | bytes 2097152 | tf_op jit(solution)/shard_map/all_to_all | solution.py:62
  42.5 1.6 copy.21
  44.0 25.9 %all-to-all-done.4 = bf16[256,8,256]{2,1,0:T(8,128)(2,1)} async-done(((bf16[256,8,256]{2,1,0:T(8,128)(2,1)}), bf16[256,8,256]{2,1,0:T(8,128)(2,1)}, u32[]{:S(2)}, u32[]{:S(2)}) %all-to-all-start.4) | async-done | bytes 1048608 | tf_op jit(solution)/shard_map/all_to_all | solution.py:62
  70.0 9.5 %all-to-all-start.1 = ((bf16[256,8,256]{2,1,0:T(8,128)(2,1)}), bf16[256,8,256]{2,1,0:T(8,128)(2,1)S(1)}, u32[]{:S(2)}, u32[]{:S(2)}) async-start(bf16[256,8,256]{2,1,0:T(8,128)(2,1)} %copy.21), calls=%async_computation.1 | async-start | bytes 2097152 | tf_op jit(solution)/shard_map/all_to_all | solution.py:62
  79.5 1.9 convolution_convert_fusion.4
  81.4 1.8 copy.29
  83.2 24.5 %all-to-all-done.1 = bf16[256,8,256]{2,1,0:T(8,128)(2,1)S(1)} async-done(((bf16[256,8,256]{2,1,0:T(8,128)(2,1)}), bf16[256,8,256]{2,1,0:T(8,128)(2,1)S(1)}, u32[]{:S(2)}, u32[]{:S(2)}) %all-to-all-start.1) | async-done | bytes 1048608 | tf_op jit(solution)/shard_map/all_to_all | solution.py:62
  107.7 9.5 %all-to-all-start.5 = ((bf16[512,4,256]{2,1,0:T(4,128)(2,1)}), bf16[512,4,256]{2,1,0:T(4,128)(2,1)S(1)}, u32[]{:S(2)}, u32[]{:S(2)}) async-start(bf16[512,4,256]{2,1,0:T(4,128)(2,1)} %copy.29), calls=%async_computation.5 | async-start | bytes 2097152 | tf_op jit(solution)/shard_map/all_to_all | solution.py:66
  117.9 1.8 copy.23
  119.7 25.8 %all-to-all-done.5 = bf16[512,4,256]{2,1,0:T(4,128)(2,1)S(1)} async-done(((bf16[512,4,256]{2,1,0:T(4,128)(2,1)}), bf16[512,4,256]{2,1,0:T(4,128)(2,1)S(1)}, u32[]{:S(2)}, u32[]{:S(2)}) %all-to-all-start.5) | async-done | bytes 1048608 | tf_op jit(solution)/shard_map/all_to_all | solution.py:66
  145.5 9.5 %all-to-all-start.2 = ((bf16[512,4,256]{2,1,0:T(4,128)(2,1)}), bf16[512,4,256]{2,1,0:T(4,128)(2,1)S(1)}, u32[]{:S(2)}, u32[]{:S(2)}) async-start(bf16[512,4,256]{2,1,0:T(4,128)(2,1)} %copy.23), calls=%async_computation.2 | async-start | bytes 2097152 | tf_op jit(solution)/shard_map/all_to_all | solution.py:66
  156.2 1.7 reshape.113
  158.0 25.4 %all-to-all-done.2 = bf16[512,4,256]{2,1,0:T(4,128)(2,1)S(1)} async-done(((bf16[512,4,256]{2,1,0:T(4,128)(2,1)}), bf16[512,4,256]{2,1,0:T(4,128)(2,1)S(1)}, u32[]{:S(2)}, u32[]{:S(2)}) %all-to-all-start.2) | async-done | bytes 1048608 | tf_op jit(solution)/shard_map/all_to_all | solution.py:66
  184.0 1.7 reshape.112
  185.8 3.4 %multiply_convert_fusion.2 = (bf16[8,256,256]{2,1,0:T(8,128)(2,1)S(1)}, bf16[8,256,256]{2,1,0:T(8,128)(2,1)S(1)}) fusion(f32[8,256,256]{2,1,0:T(8,128)} %reshape.112, bf16[8,512,256]{2,1,0:T(8,128)(2,1)} %bitcast.76, f32[8,256,256]{2,1,0:T(8,128)} %reshape.113), kind=kLoop, calls=%fused_computation.9 | loop fusion | flops 3145728 | bytes 8388608 | tf_op jit(solution)/shard_map/convert_element_type | solution.py:69
  189.2 1.5 convolution_convert_fusion.3
  190.6 3.6 %all-to-all-start.3 = ((bf16[8,32,2048]{2,1,0:T(8,128)(2,1)}), bf16[8,32,2048]{2,1,0:T(8,128)(2,1)S(1)}, u32[]{:S(2)}, u32[]{:S(2)}) async-start(bf16[8,32,2048]{2,1,0:T(8,128)(2,1)} %bitcast.15), calls=%async_computation.3 | async-start | bytes 2097152 | tf_op jit(solution)/shard_map/all_to_all | solution.py:75
  195.7 14.8 %all-to-all-done.3 = bf16[8,32,2048]{2,1,0:T(8,128)(2,1)S(1)} async-done(((bf16[8,32,2048]{2,1,0:T(8,128)(2,1)}), bf16[8,32,2048]{2,1,0:T(8,128)(2,1)S(1)}, u32[]{:S(2)}, u32[]{:S(2)}) %all-to-all-start.3) | async-done | bytes 1048608 | tf_op jit(solution)/shard_map/all_to_all | solution.py:75
  210.5 3.6 %all-to-all-start.6 = ((bf16[8,32,2048]{2,1,0:T(8,128)(2,1)}), bf16[8,32,2048]{2,1,0:T(8,128)(2,1)S(1)}, u32[]{:S(2)}, u32[]{:S(2)}) async-start(bf16[8,32,2048]{2,1,0:T(8,128)(2,1)} %bitcast.29), calls=%async_computation.6 | async-start | bytes 2097152 | tf_op jit(solution)/shard_map/all_to_all | solution.py:75
  215.1 15.7 %all-to-all-done.6 = bf16[8,32,2048]{2,1,0:T(8,128)(2,1)S(1)} async-done(((bf16[8,32,2048]{2,1,0:T(8,128)(2,1)}), bf16[8,32,2048]{2,1,0:T(8,128)(2,1)S(1)}, u32[]{:S(2)}, u32[]{:S(2)}) %all-to-all-start.6) | async-done | bytes 1048608 | tf_op jit(solution)/shard_map/all_to_all | solution.py:75
  231.3 1.5 pad_maximum_fusion
  (31 shorter events, 9.0 us)
Async XLA Ops:
  0.0 8.1 %copy-start.3 = (f32[8,512]{1,0:T(8,128)S(1)}, f32[8,512]{1,0:T(8,128)}, u32[]{:S(2)}) copy-start(f32[8,512]{1,0:T(8,128)} %param.8) | copy-start | bytes 49156
  0.9 22.9 %copy-start = (bf16[4096,256]{1,0:T(8,128)(2,1)S(1)}, bf16[4096,256]{1,0:T(8,128)(2,1)}, u32[]{:S(2)}) copy-start(bf16[4096,256]{1,0:T(8,128)(2,1)} %param.6) | copy-start | bytes 6291460
  2.0 21.8 %all-to-all-start = ((bf16[8,128,512]{2,1,0:T(8,128)(2,1)}), bf16[8,128,512]{2,1,0:T(8,128)(2,1)S(1)}, u32[]{:S(2)}, u32[]{:S(2)}) async-start(bf16[8,128,512]{2,1,0:T(8,128)(2,1)} %stack.2), calls=%async_computation | async-start | bytes 2097152 | tf_op jit(solution)/shard_map/all_to_all | solution.py:13
  26.1 43.9 %all-to-all-start.4 = ((bf16[256,8,256]{2,1,0:T(8,128)(2,1)}), bf16[256,8,256]{2,1,0:T(8,128)(2,1)}, u32[]{:S(2)}, u32[]{:S(2)}) async-start(bf16[256,8,256]{2,1,0:T(8,128)(2,1)} %copy.27), calls=%async_computation.4 | async-start | bytes 2097152 | tf_op jit(solution)/shard_map/all_to_all | solution.py:62
  70.0 37.7 %all-to-all-start.1 = ((bf16[256,8,256]{2,1,0:T(8,128)(2,1)}), bf16[256,8,256]{2,1,0:T(8,128)(2,1)S(1)}, u32[]{:S(2)}, u32[]{:S(2)}) async-start(bf16[256,8,256]{2,1,0:T(8,128)(2,1)} %copy.21), calls=%async_computation.1 | async-start | bytes 2097152 | tf_op jit(solution)/shard_map/all_to_all | solution.py:62
  107.7 37.8 %all-to-all-start.5 = ((bf16[512,4,256]{2,1,0:T(4,128)(2,1)}), bf16[512,4,256]{2,1,0:T(4,128)(2,1)S(1)}, u32[]{:S(2)}, u32[]{:S(2)}) async-start(bf16[512,4,256]{2,1,0:T(4,128)(2,1)} %copy.29), calls=%async_computation.5 | async-start | bytes 2097152 | tf_op jit(solution)/shard_map/all_to_all | solution.py:66
  117.9 37.1 %copy-start.1 = (bf16[8,32,32]{2,1,0:T(8,128)(2,1)S(1)}, bf16[8,32,32]{2,1,0:T(8,128)(2,1)}, u32[]{:S(2)}) copy-start(bf16[8,32,32]{2,1,0:T(8,128)(2,1)} %param.10) | copy-start | bytes 49156
  145.5 37.9 %all-to-all-start.2 = ((bf16[512,4,256]{2,1,0:T(4,128)(2,1)}), bf16[512,4,256]{2,1,0:T(4,128)(2,1)S(1)}, u32[]{:S(2)}, u32[]{:S(2)}) async-start(bf16[512,4,256]{2,1,0:T(4,128)(2,1)} %copy.23), calls=%async_computation.2 | async-start | bytes 2097152 | tf_op jit(solution)/shard_map/all_to_all | solution.py:66
  190.6 19.9 %all-to-all-start.3 = ((bf16[8,32,2048]{2,1,0:T(8,128)(2,1)}), bf16[8,32,2048]{2,1,0:T(8,128)(2,1)S(1)}, u32[]{:S(2)}, u32[]{:S(2)}) async-start(bf16[8,32,2048]{2,1,0:T(8,128)(2,1)} %bitcast.15), calls=%async_computation.3 | async-start | bytes 2097152 | tf_op jit(solution)/shard_map/all_to_all | solution.py:75
  194.2 19.9 %copy-start.2 = (bf16[4,64,64]{2,1,0:T(8,128)(2,1)S(1)}, bf16[4,64,64]{2,1,0:T(8,128)(2,1)}, u32[]{:S(2)}) copy-start(bf16[4,64,64]{2,1,0:T(8,128)(2,1)} %param.11) | copy-start | bytes 98308
  210.5 20.3 %all-to-all-start.6 = ((bf16[8,32,2048]{2,1,0:T(8,128)(2,1)}), bf16[8,32,2048]{2,1,0:T(8,128)(2,1)S(1)}, u32[]{:S(2)}, u32[]{:S(2)}) async-start(bf16[8,32,2048]{2,1,0:T(8,128)(2,1)} %bitcast.29), calls=%async_computation.6 | async-start | bytes 2097152 | tf_op jit(solution)/shard_map/all_to_all | solution.py:75
